TPU v7x, 512 devices: a whole 4x8x8 slice. The times are simulated.
512 devices in a mesh: dp: 2 (over core), section: 8 (over z), mem: 32 (over y, x).
Axes of the slice: x: 4, y: 8, z: 8, core: 2. Of those that a mesh axis runs over, the one named last changes fastest.
Arguments:
- qkv_rows: bfloat16 [8, 64, 128, 3072], P('section', ('dp', 'mem')), may hold values from -5 to 5
- grad_output: bfloat16 [8, 64, 128, 2048], P('section', ('dp', 'mem')), may hold values from -12 to 12
- memory_rows: bfloat16 [8, 256, 64, 1024], P('section', 'mem'), may hold values from -5 to 5
- shard_fill: int32 [8, 32], P('section', 'mem'), may hold values from 257 to 512, as said below
- block_ids: int32 [8, 64, 2, 8], P('section', ('dp', 'mem')), may hold values from 0 to 255, as said below
Outputs:
- upstream: bfloat16 [8, 64, 128, 3072], P('section', ('dp', 'mem'))
- memory_grad: bfloat16 [8, 256, 64, 1024], P('section', 'mem')
Inputs may be any that keep to these rules, and one draw needn't show every extreme that they name: `shard_fill`: memory tokens at or beyond a shard's fill are empty. In every section one shard is full and one holds 257 tokens. `block_ids`: each query block names 8 blocks of different shards; all query blocks of one sequence together name at most one distinct block of any one shard; every named block holds a live token.
All inputs are finite; a program needn't handle non-finite values.
Results may differ from a plain program's by a relative error of at most 0.011.
Values may be sent and summed in bfloat16 or wider, within the bound.
No kernel may reach another device: no remote copies, remote signals or barrier semaphores. Data moves between devices by JAX's collectives and lax.ppermute only.
A program may use at most 128 MiB of HBM per device.

v0:
```python
from functools import partial

import jax
import jax.numpy as jnp
from jax import lax
from jax.sharding import PartitionSpec as P

H = 16
KEY_VALUE_HEADS = 4
DH = 128
BLK = 64


NEG_FILL = -1e30


def passed_along(array, axis, by):
    devices = lax.axis_size(axis)
    pairs = [(i, i + by) for i in range(devices) if 0 <= i + by < devices]
    return lax.ppermute(array, axis, pairs)


def head_scores(key_mask, queries, key_rows):
    raw = jnp.einsum(
        "bihd,bnd->bihn", queries, key_rows, preferred_element_type=jnp.float32
    ) * DH ** (-0.5)
    return jnp.where(key_mask[:, :, None, :], raw, NEG_FILL)


def head_forward(key_mask, pieces):
    queries, key_rows, value_rows = pieces
    scores = head_scores(key_mask, queries, key_rows)
    row_max = jnp.max(scores, axis=-1, keepdims=True)
    log_total = row_max + jnp.log(jnp.sum(jnp.exp(scores - row_max), axis=-1, keepdims=True))
    prob_bf = jnp.exp(scores - log_total).astype(jnp.bfloat16)
    attended = jnp.einsum(
        "bihn,bnd->bihd", prob_bf, value_rows, preferred_element_type=jnp.float32
    ).astype(jnp.bfloat16)
    return (log_total, attended)


def head_backward(key_mask, pieces):
    queries, key_rows, value_rows, grad_rows, log_total, attended = pieces
    scores = head_scores(key_mask, queries, key_rows)
    weights = jnp.exp(scores - log_total)
    prob_bf = weights.astype(jnp.bfloat16)
    dprobs = jnp.einsum("bihd,bnd->bihn", grad_rows, value_rows, preferred_element_type=jnp.float32)
    row_delta = jnp.sum(
        grad_rows.astype(jnp.float32) * attended.astype(jnp.float32), axis=-1, keepdims=True
    )
    dscores = (weights * (dprobs - row_delta)).astype(jnp.bfloat16)
    inv_root = DH ** (-0.5)
    grad_query = (
        jnp.einsum("bihn,bnd->bihd", dscores, key_rows, preferred_element_type=jnp.float32)
        * inv_root
    )
    grad_key = (
        jnp.einsum("bihn,bihd->bnd", dscores, queries, preferred_element_type=jnp.float32)
        * inv_root
    )
    grad_value = jnp.einsum(
        "bihn,bihd->bnd", prob_bf, grad_rows, preferred_element_type=jnp.float32
    )
    return (grad_query, grad_key, grad_value)


def assemble(slots, slot_live, owner_shard, keys_local, values_local):
    qblocks, topk = owner_shard.shape
    tokens = keys_local.shape[0]
    width = KEY_VALUE_HEADS * DH
    memory_len = topk * BLK
    picked = jnp.take(slots, owner_shard.reshape(-1), axis=0)
    mem_keys = picked[..., :width].reshape(qblocks, memory_len, KEY_VALUE_HEADS, DH)
    mem_values = picked[..., width:].reshape(qblocks, memory_len, KEY_VALUE_HEADS, DH)
    key_rows = jnp.concatenate(
        [mem_keys, jnp.broadcast_to(keys_local[None], (qblocks, tokens, KEY_VALUE_HEADS, DH))],
        axis=1,
    )
    value_rows = jnp.concatenate(
        [mem_values, jnp.broadcast_to(values_local[None], (qblocks, tokens, KEY_VALUE_HEADS, DH))],
        axis=1,
    )
    live_len = jnp.take(slot_live[:, 0], owner_shard.reshape(-1))
    live_mask = (jnp.arange(BLK)[None, :] < live_len[:, None]).reshape(qblocks, memory_len)
    row_pos = jnp.arange(qblocks)[:, None] * BLK + jnp.arange(BLK)[None, :]
    causal = jnp.arange(tokens)[None, None, :] <= row_pos[:, :, None]
    key_mask = jnp.concatenate(
        [jnp.broadcast_to(live_mask[:, None, :], (qblocks, BLK, memory_len)), causal], axis=-1
    )
    return (
        jnp.transpose(key_rows, (2, 0, 1, 3)),
        jnp.transpose(value_rows, (2, 0, 1, 3)),
        key_mask,
    )


def per_device(qkv_rows, grad_output, memory_rows, shard_fill, block_ids):
    shards = lax.axis_size("mem")
    groups = H // KEY_VALUE_HEADS
    width = KEY_VALUE_HEADS * DH
    rows_here = qkv_rows[0, 0]
    tokens = rows_here.shape[0]
    ids_here = block_ids[0, 0]
    qblocks, topk = ids_here.shape
    memory_len = topk * BLK
    held_blocks = memory_rows.shape[1]
    queries = rows_here[:, : H * DH].reshape(qblocks, BLK, KEY_VALUE_HEADS, groups, DH)
    keys_local = rows_here[:, H * DH : (H + KEY_VALUE_HEADS) * DH].reshape(
        tokens, KEY_VALUE_HEADS, DH
    )
    values_local = rows_here[:, (H + KEY_VALUE_HEADS) * DH :].reshape(tokens, KEY_VALUE_HEADS, DH)
    grad_rows = grad_output[0, 0].reshape(qblocks, BLK, KEY_VALUE_HEADS, groups, DH)
    queries_head = jnp.transpose(queries, (2, 0, 1, 3, 4))
    grads_head = jnp.transpose(grad_rows, (2, 0, 1, 3, 4))
    owner_shard = ids_here // held_blocks
    slot_index = ids_here % held_blocks
    shard_ids = jnp.arange(shards, dtype=jnp.int32)
    hits = owner_shard[:, :, None] == shard_ids[None, None, :]
    request = jnp.max(jnp.where(hits, slot_index[:, :, None], -1), axis=(0, 1))
    wanted = lax.all_to_all(request[:, None], "mem", split_axis=0, concat_axis=0, tiled=True)[:, 0]
    picked = jnp.take(memory_rows[0], jnp.maximum(wanted, 0), axis=0)
    live_len = jnp.where(wanted >= 0, jnp.clip(shard_fill[0, 0] - wanted * BLK, 0, BLK), 0)[:, None]
    slots, slot_live = (
        lax.all_to_all(picked, "mem", split_axis=0, concat_axis=0, tiled=True),
        lax.all_to_all(live_len, "mem", split_axis=0, concat_axis=0, tiled=True),
    )
    key_rows, value_rows, key_mask = assemble(
        slots, slot_live, owner_shard, keys_local, values_local
    )
    log_total, attended = lax.map(
        partial(head_forward, key_mask), (queries_head, key_rows, value_rows)
    )
    served_again = lax.optimization_barrier((picked, live_len, log_total))
    slots_back, live_back = (
        lax.all_to_all(served_again[0], "mem", split_axis=0, concat_axis=0, tiled=True),
        lax.all_to_all(served_again[1], "mem", split_axis=0, concat_axis=0, tiled=True),
    )
    key_rows, value_rows, key_mask = assemble(
        slots_back, live_back, owner_shard, keys_local, values_local
    )
    grad_query, grad_key, grad_value = lax.map(
        partial(head_backward, key_mask),
        (queries_head, key_rows, value_rows, grads_head, log_total, attended),
    )
    query_part = jnp.transpose(grad_query, (1, 2, 0, 3, 4)).reshape(tokens, H * DH)
    local_key = jnp.transpose(jnp.sum(grad_key[:, :, memory_len:], axis=1), (1, 0, 2)).reshape(
        tokens, width
    )
    local_value = jnp.transpose(jnp.sum(grad_value[:, :, memory_len:], axis=1), (1, 0, 2)).reshape(
        tokens, width
    )
    section_grads = jnp.concatenate([query_part, local_key, local_value], axis=-1).astype(
        jnp.bfloat16
    )
    upstream = passed_along(section_grads[None, None], "section", -1)
    mem_key_grad = jnp.transpose(grad_key[:, :, :memory_len], (1, 2, 0, 3)).reshape(
        qblocks, topk, BLK * width
    )
    mem_value_grad = jnp.transpose(grad_value[:, :, :memory_len], (1, 2, 0, 3)).reshape(
        qblocks, topk, BLK * width
    )
    key_slot = jnp.sum(jnp.where(hits, jnp.arange(topk, dtype=jnp.int32)[None, :, None], 0), axis=1)
    present = jnp.any(hits, axis=1)[:, :, None, None]
    entry_grads = jnp.concatenate(
        [
            mem_key_grad.reshape(qblocks, topk, BLK, width),
            mem_value_grad.reshape(qblocks, topk, BLK, width),
        ],
        axis=-1,
    )
    placed = jnp.take_along_axis(entry_grads, key_slot[:, :, None, None], axis=1)
    slot_grads = jnp.sum(jnp.where(present, placed, jnp.float32(0.0)), axis=0).astype(jnp.bfloat16)
    received = lax.all_to_all(slot_grads, "mem", split_axis=0, concat_axis=0, tiled=True)
    wanted_hot = (wanted[:, None] == jnp.arange(held_blocks, dtype=jnp.int32)[None, :]).astype(
        jnp.bfloat16
    )
    owned = jnp.einsum(
        "rj,rx->jx",
        wanted_hot,
        received.reshape(shards, BLK * 2 * width),
        preferred_element_type=jnp.float32,
    )
    summed = lax.psum(owned, "dp")
    memory_grad = summed.astype(jnp.bfloat16).reshape(1, held_blocks, BLK, 2 * width)
    return (upstream, memory_grad)


def solution(mesh):
    placed = (
        P("section", ("dp", "mem"), None, None),
        P("section", ("dp", "mem"), None, None),
        P("section", "mem", None, None),
        P("section", "mem"),
        P("section", ("dp", "mem"), None, None),
    )
    return jax.shard_map(
        per_device,
        mesh=mesh,
        in_specs=placed,
        out_specs=(P("section", ("dp", "mem"), None, None), P("section", "mem", None, None)),
        check_vma=False,
    )
```

profile of v0, /device:TPU:1, one launch (start us, length us, event | category | flops | bytes accessed | tf_op | source)
XLA Modules:
  0.0 475.6 jit_solution(16670266246849484863)
XLA Ops:
  2.2 10.5 %all-to-all-start = ((s32[32,1,1]{2,1,0:T(1,128)}), s32[32,1,1]{2,1,0:T(1,128)S(1)}, u32[]{:S(2)}, u32[]{:S(2)}) async-start(s32[32,1,1]{2,1,0:T(1,128)} %copy.52), calls=%async_computation | async-start | bytes 32768 | tf_op jit(solution)/shard_map/all_to_all | solution.py:120
  13.4 7.9 %all-to-all-done = s32[32,1,1]{2,1,0:T(1,128)S(1)} async-done(((s32[32,1,1]{2,1,0:T(1,128)}), s32[32,1,1]{2,1,0:T(1,128)S(1)}, u32[]{:S(2)}, u32[]{:S(2)}) %all-to-all-start) | async-done | bytes 160 | tf_op jit(solution)/shard_map/all_to_all | solution.py:120
  23.5 3.8 all-to-all-start.1
  30.2 4.6 broadcast_select_fusion
  35.9 8.4 %all-to-all-start.2 = ((bf16[32,64,1024]{2,1,0:T(8,128)(2,1)}), bf16[32,64,1024]{2,1,0:T(8,128)(2,1)}, u32[]{:S(2)}, u32[]{:S(2)}) async-start(bf16[32,64,1024]{2,1,0:T(8,128)(2,1)} %broadcast_select_fusion), calls=%async_computation.2 | async-start | bytes 8388608 | tf_op jit(solution)/shard_map/all_to_all | solution.py:124
  49.0 87.9 %all-to-all-done.2 = bf16[32,64,1024]{2,1,0:T(8,128)(2,1)} async-done(((bf16[32,64,1024]{2,1,0:T(8,128)(2,1)}), bf16[32,64,1024]{2,1,0:T(8,128)(2,1)}, u32[]{:S(2)}, u32[]{:S(2)}) %all-to-all-start.2) | async-done | bytes 4194336 | tf_op jit(solution)/shard_map/all_to_all | solution.py:124
  136.9 2.9 gather_fusion.3
  145.2 15.3 %while.26 = (s32[]{:T(128)}, f32[4,2,64,4,1]{2,3,1,4,0:T(4,128)S(1)}, bf16[4,2,64,4,128]{4,2,3,1,0:T(8,128)(2,1)}, pred[2,64,640]{2,1,0:T(8,128)(4,1)S(1)}, bf16...) while((s32[]{:T(128)}, ...), condition=%wide.region_4.7_spmd, body=%wide.region_1.6_spmd.sunk | while | flops 170130944 | bytes 4958305 | solution.py:130
  160.6 14.7 %all_to_all.42 = s32[32,1,1]{2,1,0:T(1,128)S(1)} all-to-all(s32[32,1,1]{2,1,0:T(1,128)S(1)} %copy.56), channel_id=1, replica_groups=mesh['dp'=2,'section'=8,'mem'=32] {'mem'}, dimensions={0} | all-to-all | bytes 256 | tf_op jit(solution)/shard_map/all_to_all | solution.py:136
  175.3 5.2 %all-to-all-start.4 = ((bf16[32,64,1024]{2,1,0:T(8,128)(2,1)}), bf16[32,64,1024]{2,1,0:T(8,128)(2,1)}, u32[]{:S(2)}, u32[]{:S(2)}) async-start(bf16[32,64,1024]{2,1,0:T(8,128)(2,1)} %broadcast_select_fusion), calls=%async_computation.4 | async-start | bytes 8388608 | tf_op jit(solution)/shard_map/all_to_all | solution.py:135
  184.2 86.3 %all-to-all-done.4 = bf16[32,64,1024]{2,1,0:T(8,128)(2,1)} async-done(((bf16[32,64,1024]{2,1,0:T(8,128)(2,1)}), bf16[32,64,1024]{2,1,0:T(8,128)(2,1)}, u32[]{:S(2)}, u32[]{:S(2)}) %all-to-all-start.4) | async-done | bytes 4194336 | tf_op jit(solution)/shard_map/all_to_all | solution.py:135
  270.5 2.9 gather_fusion.5
  277.7 36.5 %while.27 = (s32[]{:T(128)}, bf16[4,2,64,4,128]{4,2,3,1,0:T(8,128)(2,1)}, f32[4,2,640,128]{3,2,1,0:T(8,128)}, f32[4,2,640,128]{3,2,1,0:T(8,128)}, pred[2,64,640]...) while((s32[]{:T(128)}, ...), condition=%wide.region_7.10_spmd, body=%wide.region_5.9_spmd.sunk | while | flops 422215168 | bytes 9600145 | solution.py:141
  314.2 3.9 slice_bitcast_fusion
  321.3 2.9 copy.66
  326.1 4.7 pad_maximum_fusion
  330.8 11.5 %gather_fusion.1 = f32[64,64,1024]{2,1,0:T(8,128)} fusion(f32[2,8,64,1024]{3,2,1,0:T(8,128)} %pad_maximum_fusion, s32[64]{0:T(128)S(1)} %reshape.373), kind=kCustom, calls=%fused_computation.5 | custom fusion | bytes 33554944 | tf_op jit(solution)/shard_map/jit(take_along_axis)/gather | solution.py:171
  342.3 10.5 %select_reduce_fusion = bf16[32,64,1024]{2,1,0:T(8,128)(2,1)} fusion(f32[2,32,64,1024]{3,2,1,0:T(8,128)} %bitcast.186, pred[2,32]{1,0:T(4,128)(4,1)S(1)} %compare_and_fusion.1, pred[2,32]{1,0:T(4,128)(4,1)S(1)} %fusion.45), kind=kLoop, calls=%fused_computation.60 | loop fusion | flops 10485760 | bytes 20971648 | tf_op jit(solution)/shard_map/reduce_sum | solution.py:172
  352.8 7.6 %all-to-all-start.5 = ((bf16[32,64,1024]{2,1,0:T(8,128)(2,1)}), bf16[32,64,1024]{2,1,0:T(8,128)(2,1)}, u32[]{:S(2)}, u32[]{:S(2)}) async-start(bf16[32,64,1024]{2,1,0:T(8,128)(2,1)} %select_reduce_fusion), calls=%async_computation.5 | async-start | bytes 8388608 | tf_op jit(solution)/shard_map/all_to_all | solution.py:173
  364.5 16.3 %collective-permute-done = bf16[1,1,128,3072]{3,2,1,0:T(8,128)(2,1)S(1)} collective-permute-done((bf16[1,1,128,3072]{3,2,1,0:T(8,128)(2,1)S(1)}, bf16[1,1,128,3072]{3,2,1,0:T(8,128)(2,1)S(1)}, u32[]{:S(2)}, u32[]{:S(2)}) %collective-permute-start) | collective-permute-done | bytes 786464 | tf_op jit(solution)/shard_map/ppermute | solution.py:20
  380.8 69.6 %all-to-all-done.5 = bf16[32,64,1024]{2,1,0:T(8,128)(2,1)} async-done(((bf16[32,64,1024]{2,1,0:T(8,128)(2,1)}), bf16[32,64,1024]{2,1,0:T(8,128)(2,1)}, u32[]{:S(2)}, u32[]{:S(2)}) %all-to-all-start.5) | async-done | bytes 4194336 | tf_op jit(solution)/shard_map/all_to_all | solution.py:173
  450.4 4.5 copy.76
  455.7 16.2 %all-reduce.1 = bf16[8,65536]{1,0:T(8,128)(2,1)} all-reduce(f32[8,65536]{1,0:T(8,128)S(1)} %fusion.43), channel_id=1, replica_groups=mesh['dp'=2,'section'=8,'mem'=32] {'dp'}, use_global_device_ids=true, to_apply=%region_13.16 | all-reduce | flops 524288 | bytes 3145728 | tf_op jit(solution)/shard_map/psum | solution.py:183
  471.9 2.8 copy.68
  (155 shorter events, 88.1 us)
Async XLA Ops:
  0.6 26.7 %copy-start = (bf16[1,8,64,1024]{3,2,1,0:T(8,128)(2,1)S(1)}, bf16[1,8,64,1024]{3,2,1,0:T(8,128)(2,1)}, u32[]{:S(2)}) copy-start(bf16[1,8,64,1024]{3,2,1,0:T(8,128)(2,1)} %param.15) | copy-start | bytes 3145732
  2.2 19.0 %all-to-all-start = ((s32[32,1,1]{2,1,0:T(1,128)}), s32[32,1,1]{2,1,0:T(1,128)S(1)}, u32[]{:S(2)}, u32[]{:S(2)}) async-start(s32[32,1,1]{2,1,0:T(1,128)} %copy.52), calls=%async_computation | async-start | bytes 32768 | tf_op jit(solution)/shard_map/all_to_all | solution.py:120
  23.5 12.4 %all-to-all-start.1 = ((s32[32,1,1]{2,1,0:T(1,128)}), s32[32,1,1]{2,1,0:T(1,128)S(1)}, u32[]{:S(2)}, u32[]{:S(2)}) async-start(s32[32,1,1]{2,1,0:T(1,128)} %get-tuple-element.237), calls=%async_computation.1 | async-start | bytes 32768 | tf_op jit(solution)/shard_map/all_to_all | solution.py:125
  34.8 9.5 %copy-start.11 = (s32[1,1,2,8]{3,2,1,0:T(2,128)S(1)}, s32[1,1,2,8]{3,2,1,0:T(2,128)}, u32[]{:S(2)}) copy-start(s32[1,1,2,8]{3,2,1,0:T(2,128)} %param.17) | copy-start | bytes 196
  34.8 9.7 %copy-start.6 = (bf16[1,1,128,3072]{3,2,1,0:T(8,128)(2,1)S(1)}, bf16[1,1,128,3072]{3,2,1,0:T(8,128)(2,1)}, u32[]{:S(2)}) copy-start(bf16[1,1,128,3072]{3,2,1,0:T(8,128)(2,1)} %param.13) | copy-start | bytes 2359300
  35.9 101.0 %all-to-all-start.2 = ((bf16[32,64,1024]{2,1,0:T(8,128)(2,1)}), bf16[32,64,1024]{2,1,0:T(8,128)(2,1)}, u32[]{:S(2)}, u32[]{:S(2)}) async-start(bf16[32,64,1024]{2,1,0:T(8,128)(2,1)} %broadcast_select_fusion), calls=%async_computation.2 | async-start | bytes 8388608 | tf_op jit(solution)/shard_map/all_to_all | solution.py:124
  142.5 1.6 copy-start.7
  144.1 1.0 copy-start.2
  175.3 5.3 %copy-start.8 = (bf16[1,1,128,2048]{3,2,1,0:T(8,128)(2,1)S(1)}, bf16[1,1,128,2048]{3,2,1,0:T(8,128)(2,1)}, u32[]{:S(2)}) copy-start(bf16[1,1,128,2048]{3,2,1,0:T(8,128)(2,1)} %param.14) | copy-start | bytes 1572868
  175.3 95.2 %all-to-all-start.4 = ((bf16[32,64,1024]{2,1,0:T(8,128)(2,1)}), bf16[32,64,1024]{2,1,0:T(8,128)(2,1)}, u32[]{:S(2)}, u32[]{:S(2)}) async-start(bf16[32,64,1024]{2,1,0:T(8,128)(2,1)} %broadcast_select_fusion), calls=%async_computation.4 | async-start | bytes 8388608 | tf_op jit(solution)/shard_map/all_to_all | solution.py:135
  275.1 1.6 copy-start.3
  276.7 1.0 copy-start.10
  352.8 7.6 %copy-start.9 = (bf16[4,2,64,4,128]{4,2,3,1,0:T(8,128)(2,1)S(1)}, bf16[4,2,64,4,128]{4,2,3,1,0:T(8,128)(2,1)}, u32[]{:S(2)}) copy-start(bf16[4,2,64,4,128]{4,2,3,1,0:T(8,128)(2,1)} %get-tuple-element.107) | copy-start | bytes 1572868
  352.8 97.5 %all-to-all-start.5 = ((bf16[32,64,1024]{2,1,0:T(8,128)(2,1)}), bf16[32,64,1024]{2,1,0:T(8,128)(2,1)}, u32[]{:S(2)}, u32[]{:S(2)}) async-start(bf16[32,64,1024]{2,1,0:T(8,128)(2,1)} %select_reduce_fusion), calls=%async_computation.5 | async-start | bytes 8388608 | tf_op jit(solution)/shard_map/all_to_all | solution.py:173
  363.2 17.6 %collective-permute-start = (bf16[1,1,128,3072]{3,2,1,0:T(8,128)(2,1)S(1)}, bf16[1,1,128,3072]{3,2,1,0:T(8,128)(2,1)S(1)}, u32[]{:S(2)}, u32[]{:S(2)}) collective-permute-start(bf16[1,1,128,3072]{3,2,1,0:T(8,128)(2,1)S(1)} %pad_maximum_fusion.5), channel_id=1, source_target_pairs={{32,0},{64,32},{96,64},{128,96},{160,128},{192,160},{224,192},{33,... | collective-permute-start | bytes 2359304 | tf_op jit(solution)/shard_map/ppermute | solution.py:20
  380.8 74.1 %copy-start.4 = (bf16[1,1,128,3072]{3,2,1,0:T(8,128)(2,1)}, bf16[1,1,128,3072]{3,2,1,0:T(8,128)(2,1)S(1)}, u32[]{:S(2)}) copy-start(bf16[1,1,128,3072]{3,2,1,0:T(8,128)(2,1)S(1)} %collective-permute-done) | copy-start | bytes 2359300
  455.7 20.0 %copy-start.1 = (bf16[1,8,64,1024]{3,2,1,0:T(8,128)(2,1)S(1)}, bf16[1,8,64,1024]{3,2,1,0:T(8,128)(2,1)}, u32[]{:S(2)}) copy-start(bf16[1,8,64,1024]{3,2,1,0:T(8,128)(2,1)} %param.15) | copy-start | bytes 3145732
  471.9 2.9 copy-start.5
where the time goes:
time: 477 us; the launch traced here: 476 us
  waiting for transfers between devices  269 us (56%)
  local copies, waits for them, and re-layouts  57.8 us (12%)
  matrix products  42.7 us (9%)
  starting transfers between devices  36.8 us (8%)
  other arithmetic  36.4 us (8%)
  blocking collectives  31 us (6%)
    all_to_all x1, waiting for transfers between devices, per_device(): lax.all_to_all(picked, 'mem', split_axis=0, concat_axis=0, tiled=True)  87.9 us
    all_to_all x1, waiting for transfers between devices, per_device(): lax.all_to_all(served_again[0], 'mem', split_axis=0, concat_axis=0, tiled...  86.3 us
    all_to_all x1, waiting for transfers between devices, per_device(): lax.all_to_all(slot_grads, 'mem', split_axis=0, concat_axis=0, tiled=True)  69.6 us
    ppermute x1, waiting for transfers between devices, passed_along(): return lax.ppermute(array, axis, pairs)  16.3 us
    psum x1, blocking collectives, per_device(): summed = lax.psum(owned, 'dp')  16.2 us
    all_to_all x1, blocking collectives, per_device(): lax.all_to_all(served_again[1], 'mem', split_axis=0, concat_axis=0, tiled...  14.7 us
    gather x2, local copies, waits for them, and re-layouts, per_device(): jnp.take_along_axis(entry_grads, key_slot[:, :, None, None], axis=1)  11.6 us
    dot_general x8, matrix products, head_scores(): jnp.einsum('bihd,bnd->bihn', queries, key_rows, preferred_element_type=jn...  10.8 us
  transfers between devices with their start and end apart: 6, of which 6 were waited for; matrix products, arithmetic and copies ran while one was open for 4% of the time, Pallas kernels for 0%

commit v1 on v0

--- a/solution.py
+++ b/solution.py
@@ -119,24 +119,14 @@
     request = jnp.max(jnp.where(hits, slot_index[:, :, None], -1), axis=(0, 1))
     wanted = lax.all_to_all(request[:, None], "mem", split_axis=0, concat_axis=0, tiled=True)[:, 0]
     picked = jnp.take(memory_rows[0], jnp.maximum(wanted, 0), axis=0)
-    live_len = jnp.where(wanted >= 0, jnp.clip(shard_fill[0, 0] - wanted * BLK, 0, BLK), 0)[:, None]
-    slots, slot_live = (
-        lax.all_to_all(picked, "mem", split_axis=0, concat_axis=0, tiled=True),
-        lax.all_to_all(live_len, "mem", split_axis=0, concat_axis=0, tiled=True),
-    )
+    fills = lax.all_gather(shard_fill[0, 0], "mem")
+    slot_live = jnp.where(request >= 0, jnp.clip(fills - request * BLK, 0, BLK), 0)[:, None]
+    slots = lax.all_to_all(picked, "mem", split_axis=0, concat_axis=0, tiled=True)
     key_rows, value_rows, key_mask = assemble(
         slots, slot_live, owner_shard, keys_local, values_local
     )
     log_total, attended = lax.map(
         partial(head_forward, key_mask), (queries_head, key_rows, value_rows)
-    )
-    served_again = lax.optimization_barrier((picked, live_len, log_total))
-    slots_back, live_back = (
-        lax.all_to_all(served_again[0], "mem", split_axis=0, concat_axis=0, tiled=True),
-        lax.all_to_all(served_again[1], "mem", split_axis=0, concat_axis=0, tiled=True),
-    )
-    key_rows, value_rows, key_mask = assemble(
-        slots_back, live_back, owner_shard, keys_local, values_local
     )
     grad_query, grad_key, grad_value = lax.map(
         partial(head_backward, key_mask),

time: 477 us -> 350 us (0.73)
  waiting for transfers between devices: 269 us -> 88.7 us
  blocking collectives: 31 us -> 125 us
  starting transfers between devices: 36.8 us -> 16 us
  other arithmetic: 36.4 us -> 27.9 us
  local copies, waits for them, and re-layouts: 57.8 us -> 50.8 us
  matrix products: 42.7 us -> 37.9 us
    all_to_all x3 -> x0, waiting for transfers between devices: 95.3 us -> none  [the longest x1 86.3 us: per_device(): lax.all_to_all(served_again[0], 'mem', split_axis=0, concat_axis=0, tiled...]
    all_gather x0 -> x1, blocking collectives: none -> 93.8 us  [per_device(): fills = lax.all_gather(shard_fill[0, 0], 'mem')]
    all_to_all x1, waiting for transfers between devices: 87.9 us -> 0.01 us  [per_device(): lax.all_to_all(picked, 'mem', split_axis=0, concat_axis=0, tiled=True)]
    all_to_all x3 -> x0, starting transfers between devices: 19.5 us -> none  [the longest x1 10.5 us: per_device(): lax.all_to_all(request[:, None], 'mem', split_axis=0, concat_axis=0, tile...]
    unnamed x27 -> x23, local copies, waits for them, and re-layouts: 8.3 us -> 10.1 us
  transfers between devices with their start and end apart: 6 -> 3, of which waited for: 6 -> 2; matrix products, arithmetic and copies ran while one was open for 4% -> 3% of each run, Pallas kernels for 0% -> 0%
where the time goes in v1:
time: 350 us; the launch traced here: 348 us
  blocking collectives  125 us (36%)
  waiting for transfers between devices  88.7 us (25%)
  local copies, waits for them, and re-layouts  50.8 us (15%)
  matrix products  37.9 us (11%)
  other arithmetic  27.9 us (8%)
  starting transfers between devices  16 us (5%)
    all_gather x1, blocking collectives, per_device(): fills = lax.all_gather(shard_fill[0, 0], 'mem')  93.8 us
    all_to_all x1, waiting for transfers between devices, per_device(): lax.all_to_all(slot_grads, 'mem', split_axis=0, concat_axis=0, tiled=True)  70.5 us
    all_to_all x1, blocking collectives, per_device(): lax.all_to_all(request[:, None], 'mem', split_axis=0, concat_axis=0, tile...  18.9 us
    ppermute x1, waiting for transfers between devices, passed_along(): return lax.ppermute(array, axis, pairs)  18.2 us
    psum x1, blocking collectives, per_device(): summed = lax.psum(owned, 'dp')  11.9 us
    gather x2, local copies, waits for them, and re-layouts, per_device(): jnp.take_along_axis(entry_grads, key_slot[:, :, None, None], axis=1)  11.4 us
    dot_general x8, matrix products, head_scores(): jnp.einsum('bihd,bnd->bihn', queries, key_rows, preferred_element_type=jn...  11.1 us
    reduce_sum x1, other arithmetic, per_device(): jnp.sum(jnp.where(present, placed, jnp.float32(0.0)), axis=0)  10.5 us
  transfers between devices with their start and end apart: 3, of which 2 were waited for; matrix products, arithmetic and copies ran while one was open for 3% of the time, Pallas kernels for 0%

profile of v1, /device:TPU:1, one launch (start us, length us, event | category | flops | bytes accessed | tf_op | source)
XLA Modules:
  0.0 347.8 jit_solution(3141688044733934453)
XLA Ops:
  1.6 18.9 %all_to_all.22 = s32[32,1,1]{2,1,0:T(1,128)S(1)} all-to-all(s32[32,1,1]{2,1,0:T(1,128)S(1)} %copy.50), channel_id=1, replica_groups=mesh['dp'=2,'section'=8,'mem'=32] {'mem'}, dimensions={0} | all-to-all | bytes 256 | tf_op jit(solution)/shard_map/all_to_all | solution.py:120
  21.8 2.8 gather_fusion.1
  24.6 4.6 %broadcast_select_fusion = bf16[32,64,1024]{2,1,0:T(8,128)(2,1)} fusion(bf16[32,64,1024]{2,1,0:T(8,128)(2,1)} %gather_fusion.1, pred[32]{0:T(512)(128)(4,1)S(1)} %maximum_compare_fusion), kind=kLoop, calls=%fused_computation.60 | loop fusion | flops 2097152 | bytes 8388640 | tf_op jit(solution)/shard_map/jit(_take)/select_n | solution.py:121
  29.2 5.0 %all-to-all-start.1 = ((bf16[32,64,1024]{2,1,0:T(8,128)(2,1)}), bf16[32,64,1024]{2,1,0:T(8,128)(2,1)}, u32[]{:S(2)}, u32[]{:S(2)}) async-start(bf16[32,64,1024]{2,1,0:T(8,128)(2,1)} %broadcast_select_fusion), calls=%async_computation.1 | async-start | bytes 8388608 | tf_op jit(solution)/shard_map/all_to_all | solution.py:124
  36.9 93.8 %all-reduce = s32[32]{0:T(128)S(1)} all-reduce(s32[32]{0:T(128)S(1)} %bitcast_dynamic-update-slice_fusion.1), channel_id=2, replica_groups=mesh['dp'=2,'section'=8,'mem'=32] {'mem'}, use_global_device_ids=true, to_apply=%add | all-reduce | flops 32 | bytes 256 | tf_op jit(solution)/shard_map/all_gather | solution.py:122
  134.8 2.9 gather_fusion.2
  142.4 12.9 %while.26 = (s32[]{:T(128)}, f32[4,2,64,4,1]{2,3,1,4,0:T(4,128)S(1)}, bf16[4,2,64,4,128]{4,2,3,1,0:T(8,128)(2,1)S(1)}, pred[2,64,640]{2,1,0:T(8,128)(4,1)S(1)}, ...) while((s32[]{:T(128)}, ...), condition=%wide.region_4.5_spmd, body=%wide.region_1.4_spmd.sunk | while | flops 170130944 | bytes 4960353 | solution.py:128
  155.2 30.7 %while.27 = (s32[]{:T(128)}, bf16[4,2,64,4,128]{4,2,3,1,0:T(8,128)(2,1)}, f32[4,2,640,128]{3,2,1,0:T(8,128)}, f32[4,2,640,128]{3,2,1,0:T(8,128)}, pred[2,64,640]...) while((s32[]{:T(128)}, ...), condition=%wide.region_7.8_spmd, body=%wide.region_5.7_spmd.sunk | while | flops 422215168 | bytes 13794505 | solution.py:131
  160.8 2.1 fusion.85
  168.4 2.2 fusion.85
  176.1 2.2 fusion.85
  183.8 2.2 fusion.85
  186.0 3.9 %slice_bitcast_fusion = (f32[2,512,4,128]{3,1,0,2:T(8,128)S(1)}, f32[2,512,4,128]{3,1,0,2:T(8,128)}) fusion(f32[4,2,640,128]{3,2,1,0:T(8,128)} %get-tuple-element.103, f32[4,2,640,128]{3,2,1,0:T(8,128)} %get-tuple-element.102), kind=kLoop, calls=%fused_computation.61 | loop fusion | bytes 8388608 | tf_op jit(solution)/shard_map/transpose | solution.py:149
  191.2 1.9 reshape_reshape.7
  193.1 2.9 copy.63
  197.9 4.7 %pad_maximum_fusion = f32[2,8,64,1024]{3,2,1,0:T(8,128)} fusion(f32[2,8,64,512]{3,2,1,0:T(8,128)} %reshape_reshape.7, f32[2,8,64,512]{3,2,1,0:T(8,128)} %reshape_reshape.6), kind=kLoop, calls=%fused_computation.59 | loop fusion | flops 1048576 | bytes 8388608 | tf_op jit(solution)/shard_map/concatenate | solution.py:154
  202.6 11.3 %gather_fusion.3 = f32[64,64,1024]{2,1,0:T(8,128)} fusion(f32[2,8,64,1024]{3,2,1,0:T(8,128)} %pad_maximum_fusion, s32[64]{0:T(128)S(1)} %reshape.375), kind=kCustom, calls=%fused_computation.3 | custom fusion | bytes 33554944 | tf_op jit(solution)/shard_map/jit(take_along_axis)/gather | solution.py:161
  213.9 10.5 %select_reduce_fusion = bf16[32,64,1024]{2,1,0:T(8,128)(2,1)} fusion(f32[2,32,64,1024]{3,2,1,0:T(8,128)} %bitcast.183, pred[2,32]{1,0:T(4,128)(4,1)S(1)} %compare_and_fusion, pred[2,32]{1,0:T(4,128)(4,1)S(1)} %fusion.41), kind=kLoop, calls=%fused_computation.58 | loop fusion | flops 10485760 | bytes 20971648 | tf_op jit(solution)/shard_map/reduce_sum | solution.py:162
  224.4 9.7 %all-to-all-start.2 = ((bf16[32,64,1024]{2,1,0:T(8,128)(2,1)}), bf16[32,64,1024]{2,1,0:T(8,128)(2,1)}, u32[]{:S(2)}, u32[]{:S(2)}) async-start(bf16[32,64,1024]{2,1,0:T(8,128)(2,1)} %select_reduce_fusion), calls=%async_computation.2 | async-start | bytes 8388608 | tf_op jit(solution)/shard_map/all_to_all | solution.py:163
  238.1 18.2 %collective-permute-done = bf16[1,1,128,3072]{3,2,1,0:T(8,128)(2,1)S(1)} collective-permute-done((bf16[1,1,128,3072]{3,2,1,0:T(8,128)(2,1)S(1)}, bf16[1,1,128,3072]{3,2,1,0:T(8,128)(2,1)S(1)}, u32[]{:S(2)}, u32[]{:S(2)}) %collective-permute-start) | collective-permute-done | bytes 786464 | tf_op jit(solution)/shard_map/ppermute | solution.py:20
  256.4 70.5 %all-to-all-done.2 = bf16[32,64,1024]{2,1,0:T(8,128)(2,1)} async-done(((bf16[32,64,1024]{2,1,0:T(8,128)(2,1)}), bf16[32,64,1024]{2,1,0:T(8,128)(2,1)}, u32[]{:S(2)}, u32[]{:S(2)}) %all-to-all-start.2) | async-done | bytes 4194336 | tf_op jit(solution)/shard_map/all_to_all | solution.py:163
  326.9 4.5 %copy.73 = bf16[4,8,64,1024]{3,1,2,0:T(8,128)(2,1)S(1)} copy(bf16[4,8,64,1024]{3,2,1,0:T(8,128)(2,1)} %bitcast.54) | data formatting | bytes 8388608
  332.2 11.9 %all-reduce.2 = bf16[8,65536]{1,0:T(8,128)(2,1)} all-reduce(f32[8,65536]{1,0:T(8,128)S(1)} %fusion.39), channel_id=1, replica_groups=mesh['dp'=2,'section'=8,'mem'=32] {'dp'}, use_global_device_ids=true, to_apply=%region_13.14 | all-reduce | flops 524288 | bytes 3145728 | tf_op jit(solution)/shard_map/psum | solution.py:173
  344.1 2.8 copy.65
  (146 shorter events, 56.4 us)
Async XLA Ops:
  0.6 21.1 %copy-start = (bf16[1,8,64,1024]{3,2,1,0:T(8,128)(2,1)S(1)}, bf16[1,8,64,1024]{3,2,1,0:T(8,128)(2,1)}, u32[]{:S(2)}) copy-start(bf16[1,8,64,1024]{3,2,1,0:T(8,128)(2,1)} %param.11) | copy-start | bytes 3145732
  29.2 5.0 %copy-start.10 = (s32[1,1,2,8]{3,2,1,0:T(2,128)S(1)}, s32[1,1,2,8]{3,2,1,0:T(2,128)}, u32[]{:S(2)}) copy-start(s32[1,1,2,8]{3,2,1,0:T(2,128)} %param.13) | copy-start | bytes 196
  29.2 102.6 %copy-start.5 = (bf16[1,1,128,3072]{3,2,1,0:T(8,128)(2,1)S(1)}, bf16[1,1,128,3072]{3,2,1,0:T(8,128)(2,1)}, u32[]{:S(2)}) copy-start(bf16[1,1,128,3072]{3,2,1,0:T(8,128)(2,1)} %param.9) | copy-start | bytes 2359300
  29.2 105.6 %all-to-all-start.1 = ((bf16[32,64,1024]{2,1,0:T(8,128)(2,1)}), bf16[32,64,1024]{2,1,0:T(8,128)(2,1)}, u32[]{:S(2)}, u32[]{:S(2)}) async-start(bf16[32,64,1024]{2,1,0:T(8,128)(2,1)} %broadcast_select_fusion), calls=%async_computation.1 | async-start | bytes 8388608 | tf_op jit(solution)/shard_map/all_to_all | solution.py:124
  131.7 1.5 copy-start.6
  141.3 1.0 copy-start.2
  156.4 2.8 copy-start.7
  159.5 3.4 copy-start.8
  164.0 2.8 copy-start.7
  167.1 3.4 copy-start.8
  171.7 2.8 copy-start.7
  174.8 3.5 copy-start.8
  179.4 2.8 copy-start.7
  182.5 3.5 %copy-start.8 = (bf16[4,2,64,4,128]{4,2,3,1,0:T(8,128)(2,1)}, bf16[4,2,64,4,128]{4,2,3,1,0:T(8,128)(2,1)S(1)}, u32[]{:S(2)}) copy-start(bf16[4,2,64,4,128]{4,2,3,1,0:T(8,128)(2,1)S(1)} %fusion.84) | copy-start | bytes 1572868 | tf_op jit(solution)/shard_map/while
  224.4 9.7 %copy-start.9 = (bf16[4,2,64,4,128]{4,2,3,1,0:T(8,128)(2,1)S(1)}, bf16[4,2,64,4,128]{4,2,3,1,0:T(8,128)(2,1)}, u32[]{:S(2)}) copy-start(bf16[4,2,64,4,128]{4,2,3,1,0:T(8,128)(2,1)} %get-tuple-element.101) | copy-start | bytes 1572868
  224.4 102.4 %all-to-all-start.2 = ((bf16[32,64,1024]{2,1,0:T(8,128)(2,1)}), bf16[32,64,1024]{2,1,0:T(8,128)(2,1)}, u32[]{:S(2)}, u32[]{:S(2)}) async-start(bf16[32,64,1024]{2,1,0:T(8,128)(2,1)} %select_reduce_fusion), calls=%async_computation.2 | async-start | bytes 8388608 | tf_op jit(solution)/shard_map/all_to_all | solution.py:163
  236.8 19.5 %collective-permute-start = (bf16[1,1,128,3072]{3,2,1,0:T(8,128)(2,1)S(1)}, bf16[1,1,128,3072]{3,2,1,0:T(8,128)(2,1)S(1)}, u32[]{:S(2)}, u32[]{:S(2)}) collective-permute-start(bf16[1,1,128,3072]{3,2,1,0:T(8,128)(2,1)S(1)} %pad_maximum_fusion.1), channel_id=1, source_target_pairs={{32,0},{64,32},{96,64},{128,96},{160,128},{192,160},{224,192},{33,... | collective-permute-start | bytes 2359304 | tf_op jit(solution)/shard_map/ppermute | solution.py:20
  256.4 75.0 %copy-start.3 = (bf16[1,1,128,3072]{3,2,1,0:T(8,128)(2,1)}, bf16[1,1,128,3072]{3,2,1,0:T(8,128)(2,1)S(1)}, u32[]{:S(2)}) copy-start(bf16[1,1,128,3072]{3,2,1,0:T(8,128)(2,1)S(1)} %collective-permute-done) | copy-start | bytes 2359300
  332.2 15.6 %copy-start.1 = (bf16[1,8,64,1024]{3,2,1,0:T(8,128)(2,1)S(1)}, bf16[1,8,64,1024]{3,2,1,0:T(8,128)(2,1)}, u32[]{:S(2)}) copy-start(bf16[1,8,64,1024]{3,2,1,0:T(8,128)(2,1)} %param.11) | copy-start | bytes 3145732
  344.1 2.9 copy-start.4
